TPU v7x, 32 devices: a whole 2x2x4 slice. The times are simulated.
32 devices in a mesh: grp: 4 (over y, x), blk: 8 (over z, core).
Axes of the slice: x: 2, y: 2, z: 4, core: 2. Of those that a mesh axis runs over, the one named last changes fastest.
Arguments:
- voltages: bfloat16 [4096, 188416], P(('blk', 'grp')), may hold values from -6 to 6
- filter_taps: float32 [8, 8192], replicated, may hold values from -0.0234375 to 0.0234375
- channel_index: int32 [16], replicated, may hold values from 0 to 4095
- antenna_slot_order: int32 [2048], replicated, may hold values from 0 to 2047, each once
Outputs:
- visibilities: bfloat16 [16, 4096, 2, 4096], P('grp', 'blk')
All inputs are finite; a program needn't handle non-finite values.
Results may differ from a plain program's by a relative error of at most 0.0065.
Values sent between devices are 32-bit elements; how exact they have to be, the bound alone decides.
No kernel may reach another device: no remote copies, remote signals or barrier semaphores. Data moves between devices by JAX's collectives and lax.ppermute only.
A program may use at most 192 MiB of HBM per device.

v0:
```python
import math
import jax
import jax.numpy as jnp
from jax import lax
from jax.sharding import PartitionSpec as P


def phase_table(channel_index, fft_length):
    samples_idx = jnp.arange(fft_length, dtype=jnp.int32)
    phase = samples_idx[:, None] * channel_index[None, :] % fft_length
    angle = phase.astype(jnp.float32) * jnp.float32(2.0 * math.pi / fft_length)
    return jnp.concatenate([jnp.cos(angle), -jnp.sin(angle)], axis=1).astype(jnp.bfloat16)


def channelize(voltages, filter_taps, channel_index):
    tap_count, fft_length = filter_taps.shape
    row_count = voltages.shape[0]
    frame_count = voltages.shape[1] // fft_length
    spectra = frame_count - tap_count + 1
    blocked = voltages.reshape(row_count, frame_count, fft_length)
    filtered = jnp.zeros((row_count, spectra, fft_length), jnp.float32)
    for tap_index in range(tap_count):
        filtered = filtered + filter_taps[tap_index][None, None, :] * blocked[
            :, tap_index : tap_index + spectra, :
        ].astype(jnp.float32)
    twiddle = phase_table(channel_index, fft_length)
    spectrum = jnp.dot(
        filtered.astype(jnp.bfloat16).reshape(row_count * spectra, fft_length),
        twiddle,
        preferred_element_type=jnp.float32,
    )
    chan_count = channel_index.shape[0]
    return (
        spectrum.reshape(row_count, spectra, 2, chan_count)
        .transpose(3, 2, 1, 0)
        .reshape(chan_count, 2 * spectra, row_count)
    )


def column_index(antenna_slot_order):
    count = antenna_slot_order.shape[0]
    inverse = (
        jnp.zeros((count,), jnp.int32)
        .at[antenna_slot_order]
        .set(jnp.arange(count, dtype=jnp.int32))
    )
    column_entry = jnp.arange(2 * count, dtype=jnp.int32)
    return 2 * inverse[column_entry // 2] + column_entry % 2


def stacked_rows(block):
    half = block.shape[1] // 2
    turned = jnp.concatenate([block[:, half:], -block[:, :half]], axis=1)
    return jnp.stack([block, turned], axis=1)


def correlate(lhs, cols):
    return jnp.einsum(
        "cpkr,ckn->crpn",
        lhs,
        cols,
        precision=lax.Precision.HIGHEST,
        preferred_element_type=jnp.float32,
    )


def per_device(voltages, filter_taps, channel_index, antenna_slot_order):
    local = channelize(voltages, filter_taps, channel_index)
    scale = jnp.float32(1.0 / (local.shape[1] // 2))
    columns = column_index(antenna_slot_order)
    turned = lax.all_to_all(local, "grp", split_axis=0, concat_axis=2, tiled=True)
    lhs = stacked_rows(turned)
    everything = lax.all_gather(turned, "blk", axis=2, tiled=True)
    ordered = jnp.take(everything, columns, axis=2)
    result = (correlate(lhs, ordered) * scale).astype(jnp.bfloat16)
    return result


def solution(mesh):
    in_specs = (P(("blk", "grp"), None), P(), P(), P())
    out_specs = P("grp", "blk", None, None)
    return jax.shard_map(
        per_device, mesh=mesh, in_specs=in_specs, out_specs=out_specs, check_vma=False
    )
```

profile of v0, /device:TPU:0, one launch (start us, length us, event | category | flops | bytes accessed | tf_op | source)
XLA Modules:
  0.0 413.1 jit_solution(9023769274649659987)
XLA Ops:
  6.5 0.0 all-gather.2.cloned.1.call-start
  6.5 2.3 fusion.25
  8.9 3.2 cosine_convert_fusion
  12.1 62.3 %copy.14 = bf16[128,188416]{0,1:T(8,128)(2,1)} copy(bf16[128,188416]{1,0:T(8,128)(2,1)} %param.4) | data formatting | bytes 96468992 | tf_op args[0]
  74.4 0.0 copy-start
  74.4 91.6 %fusion.4 = f32[16,2,16,128]{3,0,1,2:T(8,128)S(1)} fusion(bf16[2,16,8192,1]{2,1,0,3:T(8,128)(2,1)S(1)} %bitcast.55, bf16[128,23,8192]{0,2,1:T(8,128)(2,1)} %bitcast.49, f32[8192]{0:T(1024)S(1)} %bitcast.65, f32[8192]{0:T(1024)S(1)} %bitcast.66, f32[8192]{0:T(1024)S(1)} %bitcast.60, f32[8192]{0:T(1024)S(1)} %bitcast.61, f32[8192]{0:T(1024)S(1)} %bitcast.62, ...), kind=kOutput, calls=%fused_computation.10 | convolution fusion | flops 1476395008 | bytes 269484032 | tf_op jit(solution)/shard_map/dot_general | solution.py:27
  166.0 0.2 copy.16
  166.2 10.7 %all_to_all.18 = f32[16,32,128]{2,1,0:T(8,128)S(1)} all-to-all(f32[16,32,128]{2,1,0:T(8,128)S(1)} %bitcast.54), channel_id=1, replica_groups=mesh['grp'=4,'blk'=8] {'grp'}, dimensions={0} | all-to-all | bytes 524288 | tf_op jit(solution)/shard_map/all_to_all | solution.py:71
  176.9 0.7 copy.33
  177.6 0.0 all-gather.2.cloned.1.call-update
  177.7 0.0 copy-done
  177.7 8.2 %scatter_custom_fusion = s32[2048]{0:T(1024)S(1)} fusion(s32[2048]{0:T(1024)S(1)} %compare_select_fusion.3, s32[2048]{0:T(1024)S(1)} %iota.16, s32[]{:T(128)} %constant.59.clone.1), kind=kCustom, calls=%fused_computation.49 | custom fusion | bytes 8196 | tf_op jit(solution)/shard_map/scatter | solution.py:45
  186.0 23.0 %gather_fusion = s32[4096]{0:T(1024)S(1)} fusion(s32[2048]{0:T(1024)S(1)} %scatter_custom_fusion, s32[4096]{0:T(1024)S(1)} %broadcast_clamp_fusion.1), kind=kCustom, calls=%fused_computation | custom fusion | bytes 49152 | tf_op jit(solution)/shard_map/gather | solution.py:48
  209.1 0.2 copy.17
  209.3 0.1 stack.9
  209.4 1.0 fusion.24
  210.4 0.0 all-gather.2.cloned.1.call-done
  210.4 7.2 %copy.18 = f32[4,32,4096]{1,0,2:T(4,128)} copy(f32[4,32,4096]{2,1,0:T(8,128)} %all-gather.2.cloned.1.call-done) | data formatting | bytes 4194304 | tf_op jit(solution)/shard_map/all_gather | solution.py:73
  217.6 33.3 %gather_fusion.1 = f32[4096,4,32]{2,1,0:T(4,128)} fusion(f32[4,32,4096]{1,0,2:T(4,128)} %copy.18, s32[4096]{0:T(1024)S(1)} %broadcast_clamp_fusion), kind=kCustom, calls=%fused_computation.1 | custom fusion | bytes 4210688 | tf_op jit(solution)/shard_map/jit(_take)/gather | solution.py:74
  251.0 16.4 %select_bitcast_fusion = f32[4,32,4096,1]{1,0,2,3:T(4,128)S(1)} fusion(f32[4096,4,32]{2,1,0:T(4,128)} %gather_fusion.1, pred[4096]{0:T(1024)(128)(4,1)S(1)} %compare_and_fusion), kind=kLoop, calls=%fused_computation.9 | loop fusion | flops 524288 | bytes 4198400 | tf_op jit(solution)/shard_map/jit(_take)/select_n | solution.py:74
  267.3 57.2 %fusion.2 = bf16[4,512,2,4096]{1,3,2,0:T(8,128)(2,1)} fusion(f32[4,32,4096,1]{1,0,2,3:T(4,128)S(1)} %select_bitcast_fusion, f32[4,1,32,512]{3,2,1,0:T(8,128)S(1)} %maximum_bitcast_fusion, f32[4,1,32,512]{3,2,1,0:T(8,128)S(1)} %stack.9), kind=kOutput, calls=%fused_computation.7 | convolution fusion | flops 6476136448 | bytes 36175872 | tf_op jit(solution)/shard_map/cpkr,ckn->crpn/dot_general | solution.py:58
  324.5 81.8 %copy.21 = bf16[4,512,2,4096]{3,2,1,0:T(2,128)(2,1)} copy(bf16[4,512,2,4096]{1,3,2,0:T(8,128)(2,1)} %fusion.2) | data formatting | bytes 67108864 | tf_op jit(solution)/shard_map/convert_element_type | solution.py:75
  (10 shorter events, 0.1 us)
Async XLA Ops:
  6.5 203.9 %all-gather.2.cloned.1.call-start = ((), (), s32[]{:S(2)}) async-start(), calls=%async_computation.1 | async-start | bytes 2359296 | tf_op jit(solution)/shard_map/all_gather | solution.py:73
  74.4 103.2 %copy-start = (s32[2048]{0:T(1024)S(1)}, s32[2048]{0:T(1024)}, u32[]{:S(2)}) copy-start(s32[2048]{0:T(1024)} %param.7) | copy-start | bytes 24580
Sparse Core Ops, SparseCore 0:
  177.8 28.8 all-gather.1
where the time goes:
time: 417 us; the launch traced here: 413 us
  local copies, waits for them, and re-layouts  219 us (53%)
  matrix products  149 us (36%)
  other arithmetic  20.7 us (5%)
  between operations  13.6 us (3%)
  blocking collectives  10.7 us (3%)
    dot_general x1, matrix products, channelize(): jnp.dot(filtered.astype(jnp.bfloat16).reshape(row_count * spectra, fft_le...  91.6 us
    convert_element_type x1, local copies, waits for them, and re-layouts, per_device(): result = (correlate(lhs, ordered) * scale).astype(jnp.bfloat16)  81.8 us
    unnamed x3, local copies, waits for them, and re-layouts  62.3 us
    dot_general x1, matrix products, correlate(): jnp.einsum('cpkr,ckn->crpn', lhs, cols, precision=lax.Precision.HIGHEST,...  57.2 us
    gather x1, local copies, waits for them, and re-layouts, per_device(): ordered = jnp.take(everything, columns, axis=2)  33.3 us
    gather x1, local copies, waits for them, and re-layouts, column_index(): return 2 * inverse[column_entry // 2] + column_entry % 2  23 us
    select_n x2, other arithmetic, per_device(): ordered = jnp.take(everything, columns, axis=2)  16.4 us
    all_to_all x1, blocking collectives, per_device(): lax.all_to_all(local, 'grp', split_axis=0, concat_axis=2, tiled=True)  10.7 us
  transfers between devices with their start and end apart: 1, of which 0 were waited for; matrix products, arithmetic and copies ran while one was open for 8% of the time, Pallas kernels for 0%

commit v1 on v0

--- a/solution.py
+++ b/solution.py
@@ -68,7 +68,19 @@
     local = channelize(voltages, filter_taps, channel_index)
     scale = jnp.float32(1.0 / (local.shape[1] // 2))
     columns = column_index(antenna_slot_order)
-    turned = lax.all_to_all(local, "grp", split_axis=0, concat_axis=2, tiled=True)
+    tile_out, field_out = (lax.axis_size("grp"), lax.axis_index("grp"))
+    r1 = local.shape[0] // tile_out
+    r_now = jnp.roll(local, -field_out * r1, 0)
+    slots = [lax.slice_in_dim(r_now, 0, r1, axis=0)]
+    for j0 in range(1, tile_out):
+        z1 = lax.slice_in_dim(r_now, j0 * r1, (j0 + 1) * r1, axis=0)
+        slots.append(
+            lax.ppermute(
+                z1, axis_name="grp", perm=[(c, (c + j0) % tile_out) for c in range(tile_out)]
+            )
+        )
+    u1 = jnp.concatenate(slots[::-1], axis=2)
+    turned = jnp.roll(u1, (field_out + 1) * slots[0].shape[2], 2)
     lhs = stacked_rows(turned)
     everything = lax.all_gather(turned, "blk", axis=2, tiled=True)
     ordered = jnp.take(everything, columns, axis=2)

time: 417 us -> 409 us (0.981)
  blocking collectives: 10.7 us -> 0 us
  starting transfers between devices: 0.01 us -> 5.08 us
  local copies, waits for them, and re-layouts: 219 us -> 214 us
    all_to_all x1 -> x0, blocking collectives: 10.7 us -> none  [per_device(): lax.all_to_all(local, 'grp', split_axis=0, concat_axis=2, tiled=True)]
    ppermute x0 -> x3, starting transfers between devices: none -> 5.07 us  [per_device(): lax.ppermute(z1, axis_name='grp', perm=[(c, (c + j0) % tile_out) for c in...]
    unnamed x3 -> x10, local copies, waits for them, and re-layouts: 62.3 us -> 57.4 us
  transfers between devices with their start and end apart: 1 -> 4, of which waited for: 0 -> 3; matrix products, arithmetic and copies ran while one was open for 8% -> 8% of each run, Pallas kernels for 0% -> 0%
where the time goes in v1:
time: 409 us; the launch traced here: 406 us
  local copies, waits for them, and re-layouts  214 us (52%)
  matrix products  149 us (36%)
  other arithmetic  19.7 us (5%)
  between operations  13.6 us (3%)
  starting transfers between devices  5.08 us (1%)
  waiting for transfers between devices  4.09 us (1%)
    dot_general x1, matrix products, channelize(): jnp.dot(filtered.astype(jnp.bfloat16).reshape(row_count * spectra, fft_le...  91.6 us
    convert_element_type x1, local copies, waits for them, and re-layouts, per_device(): result = (correlate(lhs, ordered) * scale).astype(jnp.bfloat16)  81.8 us
    unnamed x10, local copies, waits for them, and re-layouts  57.4 us
    dot_general x1, matrix products, correlate(): jnp.einsum('cpkr,ckn->crpn', lhs, cols, precision=lax.Precision.HIGHEST,...  57.2 us
    gather x1, local copies, waits for them, and re-layouts, per_device(): ordered = jnp.take(everything, columns, axis=2)  33.4 us
    gather x1, local copies, waits for them, and re-layouts, column_index(): return 2 * inverse[column_entry // 2] + column_entry % 2  23 us
    select_n x2, other arithmetic, per_device(): ordered = jnp.take(everything, columns, axis=2)  16.4 us
    scatter x1, local copies, waits for them, and re-layouts, column_index(): inverse = jnp.zeros((count,), jnp.int32).at[antenna_slot_order].set(jnp.a...  8.23 us
  transfers between devices with their start and end apart: 4, of which 3 were waited for; matrix products, arithmetic and copies ran while one was open for 8% of the time, Pallas kernels for 0%

profile of v1, /device:TPU:0, one launch (start us, length us, event | category | flops | bytes accessed | tf_op | source)
XLA Modules:
  0.0 405.5 jit_solution(4017176406976142855)
XLA Ops:
  6.5 0.0 all-gather.2.cloned.1.call-start
  6.5 2.3 fusion.26
  8.9 3.2 cosine_convert_fusion
  12.1 57.3 %copy.14 = bf16[128,188416]{0,1:T(8,128)(2,1)} copy(bf16[128,188416]{1,0:T(8,128)(2,1)} %param.4) | data formatting | bytes 96468992 | tf_op args[0]
  69.4 0.0 copy-start
  69.4 91.6 %fusion.4 = f32[16,2,16,128]{3,0,1,2:T(8,128)S(1)} fusion(bf16[2,16,8192,1]{2,1,0,3:T(8,128)(2,1)S(1)} %bitcast.46, bf16[128,23,8192]{0,2,1:T(8,128)(2,1)} %bitcast.44, f32[8192]{0:T(1024)S(1)} %bitcast.56, f32[8192]{0:T(1024)S(1)} %bitcast.57, f32[8192]{0:T(1024)S(1)} %bitcast.51, f32[8192]{0:T(1024)S(1)} %bitcast.52, f32[8192]{0:T(1024)S(1)} %bitcast.53, ...), kind=kOutput, calls=%fused_computation.10 | convolution fusion | flops 1476395008 | bytes 269484032 | tf_op jit(solution)/shard_map/dot_general | solution.py:27
  161.0 0.2 copy.16
  161.2 0.1 fusion.16
  161.3 4.0 collective-permute-start
  165.2 0.0 collective-permute-start.2
  165.2 1.1 collective-permute-start.1
  166.3 1.0 collective-permute-done
  167.3 2.4 collective-permute-done.1
  169.7 0.7 collective-permute-done.2
  170.5 0.7 constant_dynamic-slice_fusion.1
  171.2 0.0 all-gather.2.cloned.1.call-update
  171.2 0.0 copy-done
  171.3 8.2 %scatter_custom_fusion = s32[2048]{0:T(1024)S(1)} fusion(s32[2048]{0:T(1024)S(1)} %compare_select_fusion.3, s32[2048]{0:T(1024)S(1)} %iota.16, s32[]{:T(128)} %constant.100.clone.1), kind=kCustom, calls=%fused_computation.59 | custom fusion | bytes 8196 | tf_op jit(solution)/shard_map/scatter | solution.py:45
  179.5 23.0 %gather_fusion = s32[4096]{0:T(1024)S(1)} fusion(s32[2048]{0:T(1024)S(1)} %scatter_custom_fusion, s32[4096]{0:T(1024)S(1)} %broadcast_clamp_fusion.1), kind=kCustom, calls=%fused_computation | custom fusion | bytes 49152 | tf_op jit(solution)/shard_map/gather | solution.py:48
  202.8 0.0 all-gather.2.cloned.1.call-done
  202.8 7.2 %copy.17 = f32[4,32,4096]{1,0,2:T(4,128)} copy(f32[4,32,4096]{2,1,0:T(8,128)} %all-gather.2.cloned.1.call-done) | data formatting | bytes 4194304 | tf_op jit(solution)/shard_map/all_gather | solution.py:85
  210.0 33.4 %gather_fusion.1 = f32[4096,4,32]{2,1,0:T(4,128)} fusion(f32[4,32,4096]{1,0,2:T(4,128)} %copy.17, s32[4096]{0:T(1024)S(1)} %broadcast_clamp_fusion), kind=kCustom, calls=%fused_computation.1 | custom fusion | bytes 4210688 | tf_op jit(solution)/shard_map/jit(_take)/gather | solution.py:86
  243.4 16.4 %select_bitcast_fusion = f32[4,32,4096,1]{1,0,2,3:T(4,128)S(1)} fusion(f32[4096,4,32]{2,1,0:T(4,128)} %gather_fusion.1, pred[4096]{0:T(1024)(128)(4,1)S(1)} %compare_and_fusion), kind=kLoop, calls=%fused_computation.9 | loop fusion | flops 524288 | bytes 4198400 | tf_op jit(solution)/shard_map/jit(_take)/select_n | solution.py:86
  259.7 57.2 %fusion.2 = bf16[4,512,2,4096]{1,3,2,0:T(8,128)(2,1)} fusion(f32[4,32,4096,1]{1,0,2,3:T(4,128)S(1)} %select_bitcast_fusion, f32[4,1,32,512]{3,2,1,0:T(8,128)S(1)} %maximum_bitcast_fusion, f32[4,1,32,512]{3,2,1,0:T(8,128)S(1)} %fusion.28), kind=kOutput, calls=%fused_computation.7 | convolution fusion | flops 6476136448 | bytes 36175872 | tf_op jit(solution)/shard_map/cpkr,ckn->crpn/dot_general | solution.py:58
  316.9 81.8 %copy.19 = bf16[4,512,2,4096]{3,2,1,0:T(2,128)(2,1)} copy(bf16[4,512,2,4096]{1,3,2,0:T(8,128)(2,1)} %fusion.2) | data formatting | bytes 67108864 | tf_op jit(solution)/shard_map/convert_element_type | solution.py:87
  (21 shorter events, 0.3 us)
Async XLA Ops:
  6.5 196.2 %all-gather.2.cloned.1.call-start = ((), (), s32[]{:S(2)}) async-start(), calls=%async_computation | async-start | bytes 2359296 | tf_op jit(solution)/shard_map/all_gather | solution.py:85
  69.4 101.8 %copy-start = (s32[2048]{0:T(1024)S(1)}, s32[2048]{0:T(1024)}, u32[]{:S(2)}) copy-start(s32[2048]{0:T(1024)} %param.7) | copy-start | bytes 24580
  161.3 6.0 %collective-permute-start = (f32[4,32,128]{2,1,0:T(8,128)S(1)}, f32[4,32,128]{2,1,0:T(8,128)S(1)}, u32[]{:S(2)}, u32[]{:S(2)}) collective-permute-start(f32[4,32,128]{2,1,0:T(8,128)S(1)} %get-tuple-element.9), channel_id=1, source_target_pairs={{0,24},{8,0},{16,8},{24,16},{1,25},{9,1},{17,9},{25,17},{2,26},{10... | collective-permute-start | bytes 196616 | tf_op jit(solution)/shard_map/ppermute | solution.py:78
  165.2 5.2 %collective-permute-start.2 = (f32[4,32,128]{2,1,0:T(8,128)S(1)}, f32[4,32,128]{2,1,0:T(8,128)S(1)}, u32[]{:S(2)}, u32[]{:S(2)}) collective-permute-start(f32[4,32,128]{2,1,0:T(8,128)S(1)} %get-tuple-element.7), channel_id=1, source_target_pairs={{0,8},{8,16},{16,24},{24,0},{1,9},{9,17},{17,25},{25,1},{2,10},{10... | collective-permute-start | bytes 196616 | tf_op jit(solution)/shard_map/ppermute | solution.py:78
  165.2 4.4 %collective-permute-start.1 = (f32[4,32,128]{2,1,0:T(8,128)S(1)}, f32[4,32,128]{2,1,0:T(8,128)S(1)}, u32[]{:S(2)}, u32[]{:S(2)}) collective-permute-start(f32[4,32,128]{2,1,0:T(8,128)S(1)} %get-tuple-element.8), channel_id=1, source_target_pairs={{0,16},{8,24},{16,0},{24,8},{1,17},{9,25},{17,1},{25,9},{2,18},{10... | collective-permute-start | bytes 196616 | tf_op jit(solution)/shard_map/ppermute | solution.py:78
Sparse Core Ops, SparseCore 0:
  171.4 29.9 all-gather.1
